TPU v7x, 32 devices: a whole 2x2x4 slice. The times are simulated.
32 devices in a mesh: group: 2 (over y), ctx: 8 (over z, x), dp: 2 (over core).
Axes of the slice: x: 2, y: 2, z: 4, core: 2. Of those that a mesh axis runs over, the one named last changes fastest.
Arguments:
- queries: bfloat16 [4, 1024, 512], P(('group', 'dp'), 'ctx'), parts along dimension 0, may hold values from -30 to 30
- key_rows: bfloat16 [4, 1024, 512], P(('group', 'dp'), 'ctx'), parts along dimension 0, may hold values from -30 to 30
- values: bfloat16 [4, 1024, 512], P(('group', 'dp'), 'ctx'), parts along dimension 0, may hold values from -6 to 6
- cotangent: bfloat16 [4, 1024, 1024], P(('group', 'dp'), 'ctx'), parts along dimension 0, may hold values from -6 to 6
- out_proj: bfloat16 [512, 1024], replicated, may hold values from -6 to 6
- conv_kernel: float32 [31, 1024], replicated, may hold values from -1.8 to 1.8
- lengths: int32 [4], P(('group', 'dp')), parts along dimension 0, may hold values from 640 to 1024, as said below
Outputs:
- grad_query: bfloat16 [4, 1024, 512], P(('group', 'dp'), 'ctx'), parts along dimension 0
- grad_key: bfloat16 [4, 1024, 512], P(('group', 'dp'), 'ctx'), parts along dimension 0
- grad_value: bfloat16 [4, 1024, 512], P(('group', 'dp'), 'ctx'), parts along dimension 0
- grad_out_proj: bfloat16 [1024, 1024], P('group'), parts along dimension 0
- grad_kernel: float32 [62, 1024], P('group'), parts along dimension 0
There are 2 independent parts, one for each index of `group`. A program takes and returns all parts, laid end to end along the dimension named above; an argument that names none is the same for every part. Nothing has to cross between parts.
Inputs may be any that keep to these rules, and one draw needn't show every extreme that they name: `lengths`: in every draw at least one recording is valid over all its 1024 frames.
All inputs are finite; a program needn't handle non-finite values.
Results may differ from a plain program's by a relative error of at most 0.014.
The roundings to bfloat16 on the way count: a program that leaves them out, or rounds other values in their place, can miss the bound.
Values may be sent and summed in bfloat16 or wider, within the bound.
No kernel may reach another device: no remote copies, remote signals or barrier semaphores. Data moves between devices by JAX's collectives and lax.ppermute only.
A program may use at most 64 MiB of HBM per device.

v0:
```python
import math
import jax
import jax.numpy as jnp
from jax import lax
from jax.sharding import PartitionSpec as P

HEADS = 8
HDIM = 64
KW = 31
REACH = 3


def passed_along(block, axis, distance):
    devices = range(lax.axis_size(axis))
    route = [(i - distance, i) for i in devices if i - distance in devices]
    return lax.ppermute(block, axis, route)


def padded(cells, sides, width):
    for axis, dim in sides:
        count = lax.axis_size(axis)
        ends = count - 1
        head = lax.slice_in_dim(cells, 0, width, axis=dim)
        tail = lax.slice_in_dim(cells, cells.shape[dim] - width, cells.shape[dim], axis=dim)
        cells = jnp.concatenate(
            [
                lax.ppermute(tail, axis, [(i, (i + 1) % count) for i in range(ends)]),
                cells,
                lax.ppermute(head, axis, [((i + 1) % count, i) for i in range(ends)]),
            ],
            axis=dim,
        )
    return cells


def collect(piece_own, shifter):
    from_below = [shifter(piece_own, distance) for distance in range(REACH, 0, -1)]
    from_above = [shifter(piece_own, -distance) for distance in range(1, REACH + 1)]
    return jnp.stack(from_below + [piece_own] + from_above, axis=0)


def give_back(partials, shifter):
    total = partials[REACH]
    for offset in range(2 * REACH + 1):
        if offset != REACH:
            total = total + shifter(partials[offset], offset - REACH)
    return total


def on_device(queries, key_rows, values, cotangent, out_proj, conv_kernel, lengths):
    tokens = queries.shape[1]
    width_heads = queries.shape[2]
    channels = out_proj.shape[1]
    span_blocks = 2 * REACH + 1
    scale_factor = 1.0 / math.sqrt(HDIM)
    halo_width = (KW - 1) // 2
    block_index = lax.axis_index("ctx")
    length_here = lengths[0]
    query_here = queries[0]
    key_here = key_rows[0]
    value_here = values[0]
    cot_here = cotangent[0]
    frames = block_index * tokens + jnp.arange(tokens, dtype=jnp.int32)
    valid_rows = frames < length_here
    key_frames = (block_index - REACH) * tokens + jnp.arange(span_blocks * tokens, dtype=jnp.int32)
    valid_keys = (key_frames >= 0) & (key_frames < length_here)

    def kv_shift(piece_rows, offset_by):
        return passed_along(piece_rows, "ctx", offset_by)

    gathered = collect(jnp.stack([key_here, value_here], axis=0), kv_shift)
    key_all = gathered[:, 0].reshape(span_blocks * tokens, HEADS, HDIM)
    value_all = gathered[:, 1].reshape(span_blocks * tokens, HEADS, HDIM)
    query_heads = query_here.reshape(tokens, HEADS, HDIM)
    scores = (
        jnp.einsum("qhd,khd->hqk", query_heads, key_all, preferred_element_type=jnp.float32)
        * scale_factor
    )
    scores = jnp.where(valid_keys[None, None, :], scores, -jnp.inf)
    row_max = jnp.max(scores, axis=2, keepdims=True)
    row_total = jnp.sum(jnp.exp(scores - row_max), axis=2, keepdims=True)
    log_total = row_max + jnp.log(row_total)
    weights = jnp.exp(scores - log_total).astype(jnp.bfloat16)
    attended = jnp.einsum("hqk,khd->qhd", weights, value_all, preferred_element_type=jnp.float32)
    attended = attended.reshape(tokens, width_heads).astype(jnp.bfloat16)
    hidden = jnp.dot(attended, out_proj, preferred_element_type=jnp.float32)
    masked = jnp.where(valid_rows[:, None], hidden, 0.0).astype(jnp.bfloat16)

    def pad_time(field_rows):
        return padded(field_rows, (("ctx", 0),), halo_width)

    padded_m = pad_time(masked)
    conv_out = jnp.zeros((tokens, channels), jnp.float32)
    for tap_index in range(KW):
        conv_out = conv_out + conv_kernel[tap_index] * padded_m[tap_index : tap_index + tokens]
    sigmoid_c = jax.nn.sigmoid(conv_out)
    grad_conv = (
        cot_here.astype(jnp.float32) * (sigmoid_c + conv_out * sigmoid_c * (1.0 - sigmoid_c))
    ).astype(jnp.bfloat16)
    padded_g = pad_time(grad_conv)
    grad_wide = grad_conv.astype(jnp.float32)
    grad_masked = jnp.zeros((tokens, channels), jnp.float32)
    kernel_terms = []
    for tap_index in range(KW):
        start_row = 2 * halo_width - tap_index
        grad_masked = (
            grad_masked + conv_kernel[tap_index] * padded_g[start_row : start_row + tokens]
        )
        kernel_terms.append(
            jnp.sum(
                padded_m[tap_index : tap_index + tokens].astype(jnp.float32) * grad_wide, axis=0
            )
        )
    kernel_local = jnp.stack(kernel_terms, axis=0)
    grad_hidden = (
        cot_here.astype(jnp.float32) + jnp.where(valid_rows[:, None], grad_masked, 0.0)
    ).astype(jnp.bfloat16)
    proj_local = lax.dot_general(
        attended, grad_hidden, (((0,), (0,)), ((), ())), preferred_element_type=jnp.float32
    )
    proj_part = lax.psum_scatter(proj_local, ("ctx", "dp"), scatter_dimension=0, tiled=True)
    proj_sum = lax.all_gather(proj_part.astype(jnp.bfloat16), ("ctx", "dp"), axis=0, tiled=True)
    kernel_sum = lax.psum(kernel_local, ("ctx", "dp"))
    grad_attended = lax.dot_general(
        grad_hidden, out_proj, (((1,), (1,)), ((), ())), preferred_element_type=jnp.float32
    ).astype(jnp.bfloat16)
    grad_heads = grad_attended.reshape(tokens, HEADS, HDIM)
    attended_heads = attended.reshape(tokens, HEADS, HDIM)
    delta_rows = jnp.sum(
        grad_heads.astype(jnp.float32) * attended_heads.astype(jnp.float32), axis=2
    )
    grad_weights = jnp.einsum(
        "qhd,khd->hqk", grad_heads, value_all, preferred_element_type=jnp.float32
    )
    grad_logits = (weights.astype(jnp.float32) * (grad_weights - delta_rows.T[:, :, None])).astype(
        jnp.bfloat16
    )
    grad_query = (
        jnp.einsum("hqk,khd->qhd", grad_logits, key_all, preferred_element_type=jnp.float32)
        * scale_factor
    )
    grad_query = grad_query.reshape(tokens, width_heads).astype(jnp.bfloat16)
    grad_key_all = (
        jnp.einsum("hqk,qhd->khd", grad_logits, query_heads, preferred_element_type=jnp.float32)
        * scale_factor
    )
    grad_value_all = jnp.einsum(
        "hqk,qhd->khd", weights, grad_heads, preferred_element_type=jnp.float32
    )
    placed = jnp.stack(
        [
            grad_key_all.reshape(span_blocks, tokens, width_heads),
            grad_value_all.reshape(span_blocks, tokens, width_heads),
        ],
        axis=1,
    )

    def grad_shift(piece_rows, offset_by):
        return passed_along(piece_rows, "ctx", offset_by)

    own_grads = give_back(placed, grad_shift)
    grad_key = own_grads[0].astype(jnp.bfloat16)
    grad_value = own_grads[1].astype(jnp.bfloat16)
    return (grad_query[None], grad_key[None], grad_value[None], proj_sum, kernel_sum)


def solution(mesh):
    return jax.shard_map(
        on_device,
        mesh=mesh,
        in_specs=(
            P(("group", "dp"), "ctx", None),
            P(("group", "dp"), "ctx", None),
            P(("group", "dp"), "ctx", None),
            P(("group", "dp"), "ctx", None),
            P(),
            P(),
            P(("group", "dp")),
        ),
        out_specs=(
            P(("group", "dp"), "ctx", None),
            P(("group", "dp"), "ctx", None),
            P(("group", "dp"), "ctx", None),
            P("group", None),
            P("group", None),
        ),
        check_vma=False,
    )
```

profile of v0, /device:TPU:8, one launch (start us, length us, event | category | flops | bytes accessed | tf_op | source)
XLA Modules:
  0.0 315.7 jit_solution(5518717356108394734)
XLA Ops:
  7.2 1.0 constant_dynamic-update-slice_fusion.1
  8.2 0.9 constant_dynamic-update-slice_fusion
  9.1 4.4 %collective-permute-start = (bf16[2,128,512]{2,1,0:T(8,128)(2,1)S(1)}, bf16[2,128,512]{2,1,0:T(8,128)(2,1)S(1)}, u32[]{:S(2)}, u32[]{:S(2)}) collective-permute-start(bf16[2,128,512]{2,1,0:T(8,128)(2,1)S(1)} %constant_dynamic-update-slice_fusion), channel_id=1, source_target_pairs={{0,6},{2,8},{4,10},{6,12},{8,14},{1,7},{3,9},{5,11},{7,13},{9,15},... | collective-permute-start | bytes 786440 | tf_op jit(solution)/shard_map/ppermute | solution.py:16
  13.6 3.5 %collective-permute-start.1 = (bf16[2,128,512]{2,1,0:T(8,128)(2,1)S(1)}, bf16[2,128,512]{2,1,0:T(8,128)(2,1)S(1)}, u32[]{:S(2)}, u32[]{:S(2)}) collective-permute-start(bf16[2,128,512]{2,1,0:T(8,128)(2,1)S(1)} %constant_dynamic-update-slice_fusion), channel_id=1, source_target_pairs={{0,4},{2,6},{4,8},{6,10},{8,12},{10,14},{1,5},{3,7},{5,9},{7,11},{... | collective-permute-start | bytes 786440 | tf_op jit(solution)/shard_map/ppermute | solution.py:16
  17.1 1.9 collective-permute-start.2
  19.0 4.8 %collective-permute-start.3 = (bf16[2,128,512]{2,1,0:T(8,128)(2,1)S(1)}, bf16[2,128,512]{2,1,0:T(8,128)(2,1)S(1)}, u32[]{:S(2)}, u32[]{:S(2)}) collective-permute-start(bf16[2,128,512]{2,1,0:T(8,128)(2,1)S(1)} %constant_dynamic-update-slice_fusion), channel_id=1, source_target_pairs={{2,0},{4,2},{6,4},{8,6},{10,8},{12,10},{14,12},{3,1},{5,3},{7,5},{... | collective-permute-start | bytes 786440 | tf_op jit(solution)/shard_map/ppermute | solution.py:16
  23.8 1.9 collective-permute-start.4
  25.7 2.0 fusion.150
  28.5 1.0 copy.26
  29.5 1.3 collective-permute-start.5
  30.9 1.5 collective-permute-done.2
  32.4 7.2 %collective-permute-done.3 = bf16[2,128,512]{2,1,0:T(8,128)(2,1)S(1)} collective-permute-done((bf16[2,128,512]{2,1,0:T(8,128)(2,1)S(1)}, bf16[2,128,512]{2,1,0:T(8,128)(2,1)S(1)}, u32[]{:S(2)}, u32[]{:S(2)}) %collective-permute-start.3) | collective-permute-done | bytes 262176 | tf_op jit(solution)/shard_map/ppermute | solution.py:16
  39.6 2.6 collective-permute-done.4
  42.2 1.0 fusion.146
  43.3 0.7 copy.25
  44.1 1.0 reshape_squeeze.9
  45.1 1.0 bitcast_reduce_fusion
  46.2 0.8 fusion.1
  47.0 0.8 fusion.3
  47.8 2.4 copy.27
  50.2 2.9 reshape_squeeze.11
  53.3 1.7 convolution_convert_fusion
  55.4 8.2 %collective-permute-start.7 = (bf16[15,1024]{1,0:T(8,128)(2,1)S(1)}, bf16[15,1024]{1,0:T(8,128)(2,1)S(1)}, u32[]{:S(2)}, u32[]{:S(2)}) collective-permute-start(bf16[15,1024]{1,0:T(8,128)(2,1)S(1)} %get-tuple-element.61), channel_id=1, source_target_pairs={{2,0},{4,2},{6,4},{8,6},{10,8},{12,10},{14,12},{3,1},{5,3},{7,5},{... | collective-permute-start | bytes 92168 | tf_op jit(solution)/shard_map/ppermute | solution.py:29
  63.6 1.9 collective-permute-start.6
  65.5 1.1 fusion.151
  66.7 3.6 %collective-permute-done.6 = bf16[15,1024]{1,0:T(8,128)(2,1)S(1)} collective-permute-done((bf16[15,1024]{1,0:T(8,128)(2,1)S(1)}, bf16[15,1024]{1,0:T(8,128)(2,1)S(1)}, u32[]{:S(2)}, u32[]{:S(2)}) %collective-permute-start.6) | collective-permute-done | bytes 30752 | tf_op jit(solution)/shard_map/ppermute | solution.py:27
  70.4 4.1 %fusion.84 = (f32[1024]{0:T(1024)}, f32[1024]{0:T(1024)}, f32[1024]{0:T(1024)}, f32[1024]{0:T(1024)}, f32[1024]{0:T(1024)}, /*index=5*/f32[1024]{0:T(1024)}, f32...) fusion(bf16[15,1024]{1,0:T(8,128)(2,1)S(1)} %collective-permute-done.7, ...), kind=kLoop, calls=%fused_computation.216 | loop fusion | flops 31841280 | bytes 1011712 | tf_op jit(solution)/shard_map/reduce_sum | solution.py:110
  74.6 1.9 collective-permute-start.9
  76.5 4.8 %collective-permute-start.8 = (bf16[15,1024]{1,0:T(8,128)(2,1)S(1)}, bf16[15,1024]{1,0:T(8,128)(2,1)S(1)}, u32[]{:S(2)}, u32[]{:S(2)}) collective-permute-start(bf16[15,1024]{1,0:T(8,128)(2,1)S(1)} %get-tuple-element.58), channel_id=1, source_target_pairs={{2,0},{4,2},{6,4},{8,6},{10,8},{12,10},{14,12},{3,1},{5,3},{7,5},{... | collective-permute-start | bytes 92168 | tf_op jit(solution)/shard_map/ppermute | solution.py:29
  81.3 1.6 collective-permute-done.8
  82.9 3.1 fusion.37
  86.7 1.8 fusion.152
  88.8 0.7 copy-done.7
  89.5 1.1 convolution_convert_fusion.1
  90.6 1.0 copy.29
  91.7 2.1 multiply_convert_fusion
  93.8 1.2 copy-done.1
  95.1 2.1 multiply_bitcast_fusion
  97.1 2.8 stack_reshape.6
  99.9 2.1 convolution_bitcast_fusion
  102.0 48.2 %reduce-scatter.2.cloned.1.call-done = f32[32,1024]{1,0:T(8,128)} async-done(((f32[512,1024]{1,0:T(8,128)}), f32[32,1024]{1,0:T(8,128)}) %reduce-scatter.2.cloned.1.call-update) | async-done | bytes 131088 | tf_op jit(solution)/shard_map/reduce_scatter | solution.py:121
  150.2 1.5 convert_element_type.366
  151.8 3.1 constant_dynamic-update-slice_fusion.3
  154.9 1.6 stack_reshape.7
  156.5 1.4 constant_dynamic-update-slice_fusion.2
  158.0 15.1 %fusion.145 = (f32[1,2,128,512]{2,0,3,1:T(1,128)}, f32[1,2,128,512]{2,0,3,1:T(1,128)}, f32[1,2,128,512]{2,0,3,1:T(1,128)}, f32[1,2,128,512]{2,0,3,1:T(1,128)}, f...) fusion(f32[7,2,128,512]{2,0,3,1:T(8,128)} %constant_dynamic-update-slice_fusion.2), kind=kLoop, calls=%fused_computation.316 | loop fusion | bytes 7340032 | tf_op jit(solution)/shard_map/slice | solution.py:46
  173.2 3.6 %collective-permute-start.15 = (f32[2,128,512]{1,2,0:T(8,128)S(1)}, f32[2,128,512]{1,2,0:T(8,128)S(1)}, u32[]{:S(2)}, u32[]{:S(2)}) collective-permute-start(f32[2,128,512]{1,2,0:T(8,128)S(1)} %bitcast.163), channel_id=1, source_target_pairs={{0,6},{2,8},{4,10},{6,12},{8,14},{1,7},{3,9},{5,11},{7,13},{9,15},... | collective-permute-start | bytes 1572872 | tf_op jit(solution)/shard_map/ppermute | solution.py:16
  178.1 2.4 collective-permute-start.14
  180.5 2.9 collective-permute-start.13
  183.4 4.2 %collective-permute-start.12 = (f32[2,128,512]{1,2,0:T(8,128)}, f32[2,128,512]{1,2,0:T(8,128)}, u32[]{:S(2)}, u32[]{:S(2)}) collective-permute-start(f32[2,128,512]{1,2,0:T(8,128)} %bitcast.54), channel_id=1, source_target_pairs={{2,0},{4,2},{6,4},{8,6},{10,8},{12,10},{14,12},{3,1},{5,3},{7,5},{... | collective-permute-start | bytes 1572872 | tf_op jit(solution)/shard_map/ppermute | solution.py:16
  187.6 2.6 collective-permute-start.11
  190.2 4.4 %collective-permute-done.15 = f32[2,128,512]{1,2,0:T(8,128)S(1)} collective-permute-done((f32[2,128,512]{1,2,0:T(8,128)S(1)}, f32[2,128,512]{1,2,0:T(8,128)S(1)}, u32[]{:S(2)}, u32[]{:S(2)}) %collective-permute-start.15) | collective-permute-done | bytes 524320 | tf_op jit(solution)/shard_map/ppermute | solution.py:16
  194.7 1.3 collective-permute-start.10
  196.6 2.7 stack.167
  199.3 1.7 fusion.5
  200.9 0.8 copy.40
  201.7 3.7 %collective-permute-done.14 = f32[2,128,512]{1,2,0:T(8,128)} collective-permute-done((f32[2,128,512]{1,2,0:T(8,128)}, f32[2,128,512]{1,2,0:T(8,128)}, u32[]{:S(2)}, u32[]{:S(2)}) %collective-permute-start.14) | collective-permute-done | bytes 524320 | tf_op jit(solution)/shard_map/ppermute | solution.py:16
  205.4 17.0 %collective-permute-done.13 = f32[2,128,512]{1,2,0:T(8,128)} collective-permute-done((f32[2,128,512]{1,2,0:T(8,128)}, f32[2,128,512]{1,2,0:T(8,128)}, u32[]{:S(2)}, u32[]{:S(2)}) %collective-permute-start.13) | collective-permute-done | bytes 524320 | tf_op jit(solution)/shard_map/ppermute | solution.py:16
  222.4 5.2 %collective-permute-done.11 = f32[2,128,512]{1,2,0:T(8,128)} collective-permute-done((f32[2,128,512]{1,2,0:T(8,128)}, f32[2,128,512]{1,2,0:T(8,128)}, u32[]{:S(2)}, u32[]{:S(2)}) %collective-permute-start.11) | collective-permute-done | bytes 524320 | tf_op jit(solution)/shard_map/ppermute | solution.py:16
  227.6 2.0 add_convert_fusion
  229.6 0.8 copy.41
  230.4 0.8 copy.42
  231.1 75.1 %all-reduce.2.cloned.1.call-done = f32[31,1024]{1,0:T(8,128)} async-done(((f32[31,1024]{1,0:T(8,128)}), f32[31,1024]{1,0:T(8,128)}) %all-reduce.2.cloned.1.call-update) | async-done | bytes 126992 | tf_op jit(solution)/shard_map/psum | solution.py:123
  306.2 2.3 copy.65
  (117 shorter events, 4.2 us)
Async XLA Ops:
  7.2 47.8 %copy-start = (bf16[512,1024]{1,0:T(8,128)(2,1)S(1)}, bf16[512,1024]{1,0:T(8,128)(2,1)}, u32[]{:S(2)}) copy-start(bf16[512,1024]{1,0:T(8,128)(2,1)} %param.11) | copy-start | bytes 3145732
  7.2 143.1 %reduce-scatter.2.cloned.1.call-start = ((), (), s32[]{:S(2)}) async-start(), calls=%async_computation.1 | async-start | bytes 2228224 | tf_op jit(solution)/shard_map/reduce_scatter | solution.py:121
  9.1 20.4 %collective-permute-start = (bf16[2,128,512]{2,1,0:T(8,128)(2,1)S(1)}, bf16[2,128,512]{2,1,0:T(8,128)(2,1)S(1)}, u32[]{:S(2)}, u32[]{:S(2)}) collective-permute-start(bf16[2,128,512]{2,1,0:T(8,128)(2,1)S(1)} %constant_dynamic-update-slice_fusion), channel_id=1, source_target_pairs={{0,6},{2,8},{4,10},{6,12},{8,14},{1,7},{3,9},{5,11},{7,13},{9,15},... | collective-permute-start | bytes 786440 | tf_op jit(solution)/shard_map/ppermute | solution.py:16
  13.6 17.3 %collective-permute-start.1 = (bf16[2,128,512]{2,1,0:T(8,128)(2,1)S(1)}, bf16[2,128,512]{2,1,0:T(8,128)(2,1)S(1)}, u32[]{:S(2)}, u32[]{:S(2)}) collective-permute-start(bf16[2,128,512]{2,1,0:T(8,128)(2,1)S(1)} %constant_dynamic-update-slice_fusion), channel_id=1, source_target_pairs={{0,4},{2,6},{4,8},{6,10},{8,12},{10,14},{1,5},{3,7},{5,9},{7,11},{... | collective-permute-start | bytes 786440 | tf_op jit(solution)/shard_map/ppermute | solution.py:16
  17.1 15.3 %collective-permute-start.2 = (bf16[2,128,512]{2,1,0:T(8,128)(2,1)S(1)}, bf16[2,128,512]{2,1,0:T(8,128)(2,1)S(1)}, u32[]{:S(2)}, u32[]{:S(2)}) collective-permute-start(bf16[2,128,512]{2,1,0:T(8,128)(2,1)S(1)} %constant_dynamic-update-slice_fusion), channel_id=1, source_target_pairs={{0,2},{2,4},{4,6},{6,8},{8,10},{10,12},{12,14},{1,3},{3,5},{5,7},{... | collective-permute-start | bytes 786440 | tf_op jit(solution)/shard_map/ppermute | solution.py:16
  19.0 20.6 %collective-permute-start.3 = (bf16[2,128,512]{2,1,0:T(8,128)(2,1)S(1)}, bf16[2,128,512]{2,1,0:T(8,128)(2,1)S(1)}, u32[]{:S(2)}, u32[]{:S(2)}) collective-permute-start(bf16[2,128,512]{2,1,0:T(8,128)(2,1)S(1)} %constant_dynamic-update-slice_fusion), channel_id=1, source_target_pairs={{2,0},{4,2},{6,4},{8,6},{10,8},{12,10},{14,12},{3,1},{5,3},{7,5},{... | collective-permute-start | bytes 786440 | tf_op jit(solution)/shard_map/ppermute | solution.py:16
  23.8 18.4 %collective-permute-start.4 = (bf16[2,128,512]{2,1,0:T(8,128)(2,1)S(1)}, bf16[2,128,512]{2,1,0:T(8,128)(2,1)S(1)}, u32[]{:S(2)}, u32[]{:S(2)}) collective-permute-start(bf16[2,128,512]{2,1,0:T(8,128)(2,1)S(1)} %constant_dynamic-update-slice_fusion), channel_id=1, source_target_pairs={{4,0},{6,2},{8,4},{10,6},{12,8},{14,10},{5,1},{7,3},{9,5},{11,7},{... | collective-permute-start | bytes 786440 | tf_op jit(solution)/shard_map/ppermute | solution.py:16
  28.4 26.5 %copy-start.42 = (pred[128]{0:T(512)(128)(4,1)}, pred[128]{0:T(512)(128)(4,1)S(1)}, u32[]{:S(2)}) copy-start(pred[128]{0:T(512)(128)(4,1)S(1)} %add_compare_fusion) | copy-start | bytes 388
  29.5 15.6 %copy-start.9 = (bf16[1,128,512]{1,2,0:T(8,128)(2,1)}, bf16[1,128,512]{1,2,0:T(8,128)(2,1)S(1)}, u32[]{:S(2)}) copy-start(bf16[1,128,512]{1,2,0:T(8,128)(2,1)S(1)} %copy.26) | copy-start | bytes 393220
  29.5 12.7 %collective-permute-start.5 = (bf16[2,128,512]{2,1,0:T(8,128)(2,1)S(1)}, bf16[2,128,512]{2,1,0:T(8,128)(2,1)S(1)}, u32[]{:S(2)}, u32[]{:S(2)}) collective-permute-start(bf16[2,128,512]{2,1,0:T(8,128)(2,1)S(1)} %constant_dynamic-update-slice_fusion), channel_id=1, source_target_pairs={{6,0},{8,2},{10,4},{12,6},{14,8},{7,1},{9,3},{11,5},{13,7},{15,9},... | collective-permute-start | bytes 786440 | tf_op jit(solution)/shard_map/ppermute | solution.py:16
  45.1 1.1 copy-start.3
  53.2 17.1 %copy-start.11 = (bf16[1,128,1024]{2,1,0:T(8,128)(2,1)S(1)}, bf16[1,128,1024]{2,1,0:T(8,128)(2,1)}, u32[]{:S(2)}) copy-start(bf16[1,128,1024]{2,1,0:T(8,128)(2,1)} %param.10) | copy-start | bytes 786436
  53.2 17.1 %copy-start.18 = (f32[1,1024]{1,0:T(1,128)S(1)}, f32[1,1024]{1,0:T(1,128)}, u32[]{:S(2)}) copy-start(f32[1,1024]{1,0:T(1,128)} %get-tuple-element.66) | copy-start | bytes 12292
  53.2 17.1 %copy-start.19 = (f32[1,1024]{1,0:T(1,128)S(1)}, f32[1,1024]{1,0:T(1,128)}, u32[]{:S(2)}) copy-start(f32[1,1024]{1,0:T(1,128)} %get-tuple-element.67) | copy-start | bytes 12292
  53.2 17.1 %copy-start.20 = (f32[1,1024]{1,0:T(1,128)S(1)}, f32[1,1024]{1,0:T(1,128)}, u32[]{:S(2)}) copy-start(f32[1,1024]{1,0:T(1,128)} %get-tuple-element.68) | copy-start | bytes 12292
  53.2 17.1 %copy-start.21 = (f32[1,1024]{1,0:T(1,128)S(1)}, f32[1,1024]{1,0:T(1,128)}, u32[]{:S(2)}) copy-start(f32[1,1024]{1,0:T(1,128)} %get-tuple-element.69) | copy-start | bytes 12292
  53.2 17.1 %copy-start.22 = (f32[1,1024]{1,0:T(1,128)S(1)}, f32[1,1024]{1,0:T(1,128)}, u32[]{:S(2)}) copy-start(f32[1,1024]{1,0:T(1,128)} %get-tuple-element.70) | copy-start | bytes 12292
  53.2 17.1 %copy-start.23 = (f32[1,1024]{1,0:T(1,128)S(1)}, f32[1,1024]{1,0:T(1,128)}, u32[]{:S(2)}) copy-start(f32[1,1024]{1,0:T(1,128)} %get-tuple-element.71) | copy-start | bytes 12292
  53.2 17.1 %copy-start.24 = (f32[1,1024]{1,0:T(1,128)S(1)}, f32[1,1024]{1,0:T(1,128)}, u32[]{:S(2)}) copy-start(f32[1,1024]{1,0:T(1,128)} %get-tuple-element.72) | copy-start | bytes 12292
  53.2 17.1 %copy-start.25 = (f32[1,1024]{1,0:T(1,128)S(1)}, f32[1,1024]{1,0:T(1,128)}, u32[]{:S(2)}) copy-start(f32[1,1024]{1,0:T(1,128)} %get-tuple-element.73) | copy-start | bytes 12292
  53.2 17.1 %copy-start.26 = (f32[1,1024]{1,0:T(1,128)S(1)}, f32[1,1024]{1,0:T(1,128)}, u32[]{:S(2)}) copy-start(f32[1,1024]{1,0:T(1,128)} %get-tuple-element.74) | copy-start | bytes 12292
  53.2 17.1 %copy-start.27 = (f32[1,1024]{1,0:T(1,128)S(1)}, f32[1,1024]{1,0:T(1,128)}, u32[]{:S(2)}) copy-start(f32[1,1024]{1,0:T(1,128)} %get-tuple-element.75) | copy-start | bytes 12292
  53.2 17.1 %copy-start.28 = (f32[1,1024]{1,0:T(1,128)S(1)}, f32[1,1024]{1,0:T(1,128)}, u32[]{:S(2)}) copy-start(f32[1,1024]{1,0:T(1,128)} %get-tuple-element.76) | copy-start | bytes 12292
  53.2 17.1 %copy-start.29 = (f32[1,1024]{1,0:T(1,128)S(1)}, f32[1,1024]{1,0:T(1,128)}, u32[]{:S(2)}) copy-start(f32[1,1024]{1,0:T(1,128)} %get-tuple-element.77) | copy-start | bytes 12292
  53.3 17.1 %copy-start.30 = (f32[1,1024]{1,0:T(1,128)S(1)}, f32[1,1024]{1,0:T(1,128)}, u32[]{:S(2)}) copy-start(f32[1,1024]{1,0:T(1,128)} %get-tuple-element.78) | copy-start | bytes 12292
  53.3 17.1 %copy-start.31 = (f32[1,1024]{1,0:T(1,128)S(1)}, f32[1,1024]{1,0:T(1,128)}, u32[]{:S(2)}) copy-start(f32[1,1024]{1,0:T(1,128)} %get-tuple-element.79) | copy-start | bytes 12292
  53.3 17.1 %copy-start.32 = (f32[1,1024]{1,0:T(1,128)S(1)}, f32[1,1024]{1,0:T(1,128)}, u32[]{:S(2)}) copy-start(f32[1,1024]{1,0:T(1,128)} %get-tuple-element.80) | copy-start | bytes 12292
  55.3 33.2 %copy-start.4 = (bf16[128,1024]{1,0:T(8,128)(2,1)}, bf16[128,1024]{1,0:T(8,128)(2,1)S(1)}, u32[]{:S(2)}) copy-start(bf16[128,1024]{1,0:T(8,128)(2,1)S(1)} %fusion.4) | copy-start | bytes 786436
  55.4 11.3 %collective-permute-start.7 = (bf16[15,1024]{1,0:T(8,128)(2,1)S(1)}, bf16[15,1024]{1,0:T(8,128)(2,1)S(1)}, u32[]{:S(2)}, u32[]{:S(2)}) collective-permute-start(bf16[15,1024]{1,0:T(8,128)(2,1)S(1)} %get-tuple-element.61), channel_id=1, source_target_pairs={{2,0},{4,2},{6,4},{8,6},{10,8},{12,10},{14,12},{3,1},{5,3},{7,5},{... | collective-permute-start | bytes 92168 | tf_op jit(solution)/shard_map/ppermute | solution.py:29
  63.6 6.7 %collective-permute-start.6 = (bf16[15,1024]{1,0:T(8,128)(2,1)S(1)}, bf16[15,1024]{1,0:T(8,128)(2,1)S(1)}, u32[]{:S(2)}, u32[]{:S(2)}) collective-permute-start(bf16[15,1024]{1,0:T(8,128)(2,1)S(1)} %get-tuple-element.60), channel_id=1, source_target_pairs={{0,2},{2,4},{4,6},{6,8},{8,10},{10,12},{12,14},{1,3},{3,5},{5,7},{... | collective-permute-start | bytes 92168 | tf_op jit(solution)/shard_map/ppermute | solution.py:27
  66.6 19.4 %copy-start.15 = (bf16[15,1024]{1,0:T(8,128)(2,1)}, bf16[15,1024]{1,0:T(8,128)(2,1)S(1)}, u32[]{:S(2)}) copy-start(bf16[15,1024]{1,0:T(8,128)(2,1)S(1)} %collective-permute-done.7) | copy-start | bytes 92164
  70.3 15.7 %copy-start.13 = (bf16[15,1024]{1,0:T(8,128)(2,1)}, bf16[15,1024]{1,0:T(8,128)(2,1)S(1)}, u32[]{:S(2)}) copy-start(bf16[15,1024]{1,0:T(8,128)(2,1)S(1)} %collective-permute-done.6) | copy-start | bytes 92164
  74.6 6.8 %collective-permute-start.9 = (bf16[15,1024]{1,0:T(8,128)(2,1)S(1)}, bf16[15,1024]{1,0:T(8,128)(2,1)S(1)}, u32[]{:S(2)}, u32[]{:S(2)}) collective-permute-start(bf16[15,1024]{1,0:T(8,128)(2,1)S(1)} %get-tuple-element.59), channel_id=1, source_target_pairs={{0,2},{2,4},{4,6},{6,8},{8,10},{10,12},{12,14},{1,3},{3,5},{5,7},{... | collective-permute-start | bytes 92168 | tf_op jit(solution)/shard_map/ppermute | solution.py:27
  76.5 6.4 %collective-permute-start.8 = (bf16[15,1024]{1,0:T(8,128)(2,1)S(1)}, bf16[15,1024]{1,0:T(8,128)(2,1)S(1)}, u32[]{:S(2)}, u32[]{:S(2)}) collective-permute-start(bf16[15,1024]{1,0:T(8,128)(2,1)S(1)} %get-tuple-element.58), channel_id=1, source_target_pairs={{2,0},{4,2},{6,4},{8,6},{10,8},{12,10},{14,12},{3,1},{5,3},{7,5},{... | collective-permute-start | bytes 92168 | tf_op jit(solution)/shard_map/ppermute | solution.py:29
  86.0 0.7 copy-start.6
  88.5 1.0 copy-start.7
  88.5 142.6 %all-gather.2.cloned.1.call-start = ((), (), s32[]{:S(2)}) async-start(), calls=%async_computation.2 | async-start | bytes 1114112 | tf_op jit(solution)/shard_map/all_gather | solution.py:122
  91.7 3.4 %copy-start.10 = (bf16[1,128,512]{1,2,0:T(8,128)(2,1)S(1)}, bf16[1,128,512]{1,2,0:T(8,128)(2,1)}, u32[]{:S(2)}) copy-start(bf16[1,128,512]{1,2,0:T(8,128)(2,1)} %copy-done.9) | copy-start | bytes 393220
  93.8 1.2 copy-start.1
  151.8 154.4 %all-reduce.2.cloned.1.call-start = ((), (), s32[]{:S(2)}) async-start(), calls=%async_computation.3 | async-start | bytes 262144 | tf_op jit(solution)/shard_map/psum | solution.py:123
  158.0 18.9 %copy-start.5 = (bf16[128,1024]{1,0:T(8,128)(2,1)S(1)}, bf16[128,1024]{1,0:T(8,128)(2,1)}, u32[]{:S(2)}) copy-start(bf16[128,1024]{1,0:T(8,128)(2,1)} %copy-done.4) | copy-start | bytes 786436
  158.0 18.9 %copy-start.16 = (bf16[15,1024]{1,0:T(8,128)(2,1)S(1)}, bf16[15,1024]{1,0:T(8,128)(2,1)}, u32[]{:S(2)}) copy-start(bf16[15,1024]{1,0:T(8,128)(2,1)} %copy-done.15) | copy-start | bytes 92164
  158.0 19.5 %copy-start.14 = (bf16[15,1024]{1,0:T(8,128)(2,1)S(1)}, bf16[15,1024]{1,0:T(8,128)(2,1)}, u32[]{:S(2)}) copy-start(bf16[15,1024]{1,0:T(8,128)(2,1)} %copy-done.13) | copy-start | bytes 92164
  173.1 23.4 %copy-start.33 = (f32[1024]{0:T(1024)S(1)}, f32[1024]{0:T(1024)}, u32[]{:S(2)}) copy-start(f32[1024]{0:T(1024)} %get-tuple-element.15) | copy-start | bytes 12292
  173.1 23.4 %copy-start.34 = (f32[1024]{0:T(1024)S(1)}, f32[1024]{0:T(1024)}, u32[]{:S(2)}) copy-start(f32[1024]{0:T(1024)} %get-tuple-element.16) | copy-start | bytes 12292
  173.1 23.4 %copy-start.35 = (f32[1024]{0:T(1024)S(1)}, f32[1024]{0:T(1024)}, u32[]{:S(2)}) copy-start(f32[1024]{0:T(1024)} %get-tuple-element.17) | copy-start | bytes 12292
  173.1 23.4 %copy-start.36 = (f32[1024]{0:T(1024)S(1)}, f32[1024]{0:T(1024)}, u32[]{:S(2)}) copy-start(f32[1024]{0:T(1024)} %get-tuple-element.18) | copy-start | bytes 12292
  173.1 23.4 %copy-start.37 = (f32[1024]{0:T(1024)S(1)}, f32[1024]{0:T(1024)}, u32[]{:S(2)}) copy-start(f32[1024]{0:T(1024)} %get-tuple-element.19) | copy-start | bytes 12292
  173.1 23.4 %copy-start.38 = (f32[1024]{0:T(1024)S(1)}, f32[1024]{0:T(1024)}, u32[]{:S(2)}) copy-start(f32[1024]{0:T(1024)} %get-tuple-element.20) | copy-start | bytes 12292
  173.1 23.4 %copy-start.39 = (f32[1024]{0:T(1024)S(1)}, f32[1024]{0:T(1024)}, u32[]{:S(2)}) copy-start(f32[1024]{0:T(1024)} %get-tuple-element.21) | copy-start | bytes 12292
  173.2 23.4 %copy-start.40 = (f32[1024]{0:T(1024)S(1)}, f32[1024]{0:T(1024)}, u32[]{:S(2)}) copy-start(f32[1024]{0:T(1024)} %get-tuple-element.22) | copy-start | bytes 12292
  173.2 23.4 %copy-start.41 = (f32[1024]{0:T(1024)S(1)}, f32[1024]{0:T(1024)}, u32[]{:S(2)}) copy-start(f32[1024]{0:T(1024)} %get-tuple-element.23) | copy-start | bytes 12292
  173.2 26.1 %copy-start.2 = (bf16[8,128,896]{1,2,0:T(8,128)(2,1)S(1)}, bf16[8,128,896]{1,2,0:T(8,128)(2,1)}, u32[]{:S(2)}) copy-start(bf16[8,128,896]{1,2,0:T(8,128)(2,1)} %copy-done.1) | copy-start | bytes 5505028
  173.2 21.5 %collective-permute-start.15 = (f32[2,128,512]{1,2,0:T(8,128)S(1)}, f32[2,128,512]{1,2,0:T(8,128)S(1)}, u32[]{:S(2)}, u32[]{:S(2)}) collective-permute-start(f32[2,128,512]{1,2,0:T(8,128)S(1)} %bitcast.163), channel_id=1, source_target_pairs={{0,6},{2,8},{4,10},{6,12},{8,14},{1,7},{3,9},{5,11},{7,13},{9,15},... | collective-permute-start | bytes 1572872 | tf_op jit(solution)/shard_map/ppermute | solution.py:16
  178.1 27.3 %collective-permute-start.14 = (f32[2,128,512]{1,2,0:T(8,128)}, f32[2,128,512]{1,2,0:T(8,128)}, u32[]{:S(2)}, u32[]{:S(2)}) collective-permute-start(f32[2,128,512]{1,2,0:T(8,128)} %bitcast.56), channel_id=1, source_target_pairs={{0,4},{2,6},{4,8},{6,10},{8,12},{10,14},{1,5},{3,7},{5,9},{7,11},{... | collective-permute-start | bytes 1572872 | tf_op jit(solution)/shard_map/ppermute | solution.py:16
  180.5 41.9 %collective-permute-start.13 = (f32[2,128,512]{1,2,0:T(8,128)}, f32[2,128,512]{1,2,0:T(8,128)}, u32[]{:S(2)}, u32[]{:S(2)}) collective-permute-start(f32[2,128,512]{1,2,0:T(8,128)} %bitcast.55), channel_id=1, source_target_pairs={{0,2},{2,4},{4,6},{6,8},{8,10},{10,12},{12,14},{1,3},{3,5},{5,7},{... | collective-permute-start | bytes 1572872 | tf_op jit(solution)/shard_map/ppermute | solution.py:16
  183.4 38.9 %collective-permute-start.12 = (f32[2,128,512]{1,2,0:T(8,128)}, f32[2,128,512]{1,2,0:T(8,128)}, u32[]{:S(2)}, u32[]{:S(2)}) collective-permute-start(f32[2,128,512]{1,2,0:T(8,128)} %bitcast.54), channel_id=1, source_target_pairs={{2,0},{4,2},{6,4},{8,6},{10,8},{12,10},{14,12},{3,1},{5,3},{7,5},{... | collective-permute-start | bytes 1572872 | tf_op jit(solution)/shard_map/ppermute | solution.py:16
  187.6 40.0 %collective-permute-start.11 = (f32[2,128,512]{1,2,0:T(8,128)}, f32[2,128,512]{1,2,0:T(8,128)}, u32[]{:S(2)}, u32[]{:S(2)}) collective-permute-start(f32[2,128,512]{1,2,0:T(8,128)} %bitcast.53), channel_id=1, source_target_pairs={{4,0},{6,2},{8,4},{10,6},{12,8},{14,10},{5,1},{7,3},{9,5},{11,7},{... | collective-permute-start | bytes 1572872 | tf_op jit(solution)/shard_map/ppermute | solution.py:16
  194.6 1.8 copy-start.12
  194.7 32.9 %collective-permute-start.10 = (f32[2,128,512]{1,2,0:T(8,128)}, f32[2,128,512]{1,2,0:T(8,128)}, u32[]{:S(2)}, u32[]{:S(2)}) collective-permute-start(f32[2,128,512]{1,2,0:T(8,128)} %bitcast.52), channel_id=1, source_target_pairs={{6,0},{8,2},{10,4},{12,6},{14,8},{7,1},{9,3},{11,5},{13,7},{15,9},... | collective-permute-start | bytes 1572872 | tf_op jit(solution)/shard_map/ppermute | solution.py:16
  196.5 31.1 %copy-start.8 = (f32[1,2,128,512]{2,0,3,1:T(1,128)S(1)}, f32[1,2,128,512]{2,0,3,1:T(1,128)}, u32[]{:S(2)}) copy-start(f32[1,2,128,512]{2,0,3,1:T(1,128)} %get-tuple-element.51) | copy-start | bytes 1572868
  306.2 2.3 copy-start.17
Sparse Core Ops, SparseCore 0:
  88.7 61.5 reduce-scatter.1
  152.4 39.2 all-gather.1
  199.4 106.7 all-reduce.1
where the time goes:
time: 317 us; the launch traced here: 316 us
  waiting for transfers between devices  170 us (54%)
  starting transfers between devices  52 us (16%)
  local copies, waits for them, and re-layouts  50.2 us (16%)
  between operations  15.3 us (5%)
  other arithmetic  14.2 us (4%)
  matrix products  13.9 us (4%)
    psum x1, waiting for transfers between devices, on_device(): kernel_sum = lax.psum(kernel_local, ('ctx', 'dp'))  75.1 us
    reduce_scatter x1, waiting for transfers between devices, on_device(): lax.psum_scatter(proj_local, ('ctx', 'dp'), scatter_dimension=0, tiled=True)  48.2 us
    ppermute x12, waiting for transfers between devices, passed_along(): return lax.ppermute(block, axis, route)  41.6 us
    ppermute x12, starting transfers between devices, passed_along(): return lax.ppermute(block, axis, route)  34.9 us
    slice x1, local copies, waits for them, and re-layouts, give_back(): total = total + shifter(partials[offset], offset - REACH)  15.1 us
    unnamed x100, local copies, waits for them, and re-layouts  13.3 us
    ppermute x2, starting transfers between devices, padded(): lax.ppermute(head, axis, [((i + 1) % count, i) for i in range(ends)])  13 us
  transfers between devices with their start and end apart: 19, of which 11 were waited for; matrix products, arithmetic and copies ran while one was open for 15% of the time, Pallas kernels for 0%

commit v1 on v0

--- a/solution.py
+++ b/solution.py
@@ -8,6 +8,11 @@
 HDIM = 64
 KW = 31
 REACH = 3
+
+
+def blocks_remake(inp):
+    tall = jnp.sum(lax.all_gather(inp, ("ctx", "dp")), axis=0)
+    return tall
 
 
 def passed_along(block, axis, distance):
@@ -120,7 +125,7 @@
     )
     proj_part = lax.psum_scatter(proj_local, ("ctx", "dp"), scatter_dimension=0, tiled=True)
     proj_sum = lax.all_gather(proj_part.astype(jnp.bfloat16), ("ctx", "dp"), axis=0, tiled=True)
-    kernel_sum = lax.psum(kernel_local, ("ctx", "dp"))
+    kernel_sum = blocks_remake(kernel_local)
     grad_attended = lax.dot_general(
         grad_hidden, out_proj, (((1,), (1,)), ((), ())), preferred_element_type=jnp.float32
     ).astype(jnp.bfloat16)

time: 317 us -> 270 us (0.85)
  waiting for transfers between devices: 170 us -> 113 us
  other arithmetic: 14.2 us -> 21.4 us
    psum x1 -> x0, waiting for transfers between devices: 75.1 us -> none  [on_device(): kernel_sum = lax.psum(kernel_local, ('ctx', 'dp'))]
    all_gather x1, waiting for transfers between devices: 0.01 us -> 29.4 us  [on_device(): lax.all_gather(proj_part.astype(jnp.bfloat16), ('ctx', 'dp'), axis=0, til...]
    reduce_scatter x1, waiting for transfers between devices: 48.2 us -> 30.6 us  [on_device(): lax.psum_scatter(proj_local, ('ctx', 'dp'), scatter_dimension=0, tiled=True)]
    ppermute x12, waiting for transfers between devices: 41.6 us -> 47.8 us  [passed_along(): return lax.ppermute(block, axis, route)]
    reduce_sum x4, other arithmetic: 5.85 us -> 10.7 us  [on_device(): jnp.sum(padded_m[tap_index:tap_index + tokens].astype(jnp.float32) * grad...]
    unnamed x100 -> x81, local copies, waits for them, and re-layouts: 13.3 us -> 11.2 us
  transfers between devices with their start and end apart: 19 -> 19, of which waited for: 11 -> 11; matrix products, arithmetic and copies ran while one was open for 15% -> 22% of each run, Pallas kernels for 0% -> 0%
where the time goes in v1:
time: 270 us; the launch traced here: 266 us
  waiting for transfers between devices  113 us (42%)
  starting transfers between devices  52 us (19%)
  local copies, waits for them, and re-layouts  51.3 us (19%)
  other arithmetic  21.4 us (8%)
  between operations  15.1 us (6%)
  matrix products  13 us (5%)
    ppermute x12, waiting for transfers between devices, passed_along(): return lax.ppermute(block, axis, route)  47.8 us
    ppermute x12, starting transfers between devices, passed_along(): return lax.ppermute(block, axis, route)  34.8 us
    reduce_scatter x1, waiting for transfers between devices, on_device(): lax.psum_scatter(proj_local, ('ctx', 'dp'), scatter_dimension=0, tiled=True)  30.6 us
    all_gather x1, waiting for transfers between devices, on_device(): lax.all_gather(proj_part.astype(jnp.bfloat16), ('ctx', 'dp'), axis=0, til...  29.4 us
    slice x1, local copies, waits for them, and re-layouts, give_back(): total = total + shifter(partials[offset], offset - REACH)  15.1 us
    ppermute x2, starting transfers between devices, padded(): lax.ppermute(head, axis, [((i + 1) % count, i) for i in range(ends)])  13 us
    unnamed x81, local copies, waits for them, and re-layouts  11.2 us
    reduce_sum x4, other arithmetic, on_device(): jnp.sum(padded_m[tap_index:tap_index + tokens].astype(jnp.float32) * grad...  10.7 us
  transfers between devices with their start and end apart: 19, of which 11 were waited for; matrix products, arithmetic and copies ran while one was open for 22% of the time, Pallas kernels for 0%

profile of v1, /device:TPU:8, one launch (start us, length us, event | category | flops | bytes accessed | tf_op | source)
XLA Modules:
  0.0 265.9 jit_solution(17418342943907672649)
XLA Ops:
  7.2 1.0 constant_dynamic-update-slice_fusion.1
  8.2 0.9 constant_dynamic-update-slice_fusion
  9.1 4.4 %collective-permute-start = (bf16[2,128,512]{2,1,0:T(8,128)(2,1)S(1)}, bf16[2,128,512]{2,1,0:T(8,128)(2,1)S(1)}, u32[]{:S(2)}, u32[]{:S(2)}) collective-permute-start(bf16[2,128,512]{2,1,0:T(8,128)(2,1)S(1)} %constant_dynamic-update-slice_fusion), channel_id=1, source_target_pairs={{0,6},{2,8},{4,10},{6,12},{8,14},{1,7},{3,9},{5,11},{7,13},{9,15},... | collective-permute-start | bytes 786440 | tf_op jit(solution)/shard_map/ppermute | solution.py:21
  13.6 3.5 %collective-permute-start.1 = (bf16[2,128,512]{2,1,0:T(8,128)(2,1)S(1)}, bf16[2,128,512]{2,1,0:T(8,128)(2,1)S(1)}, u32[]{:S(2)}, u32[]{:S(2)}) collective-permute-start(bf16[2,128,512]{2,1,0:T(8,128)(2,1)S(1)} %constant_dynamic-update-slice_fusion), channel_id=1, source_target_pairs={{0,4},{2,6},{4,8},{6,10},{8,12},{10,14},{1,5},{3,7},{5,9},{7,11},{... | collective-permute-start | bytes 786440 | tf_op jit(solution)/shard_map/ppermute | solution.py:21
  17.1 1.9 collective-permute-start.2
  19.0 4.8 %collective-permute-start.3 = (bf16[2,128,512]{2,1,0:T(8,128)(2,1)S(1)}, bf16[2,128,512]{2,1,0:T(8,128)(2,1)S(1)}, u32[]{:S(2)}, u32[]{:S(2)}) collective-permute-start(bf16[2,128,512]{2,1,0:T(8,128)(2,1)S(1)} %constant_dynamic-update-slice_fusion), channel_id=1, source_target_pairs={{2,0},{4,2},{6,4},{8,6},{10,8},{12,10},{14,12},{3,1},{5,3},{7,5},{... | collective-permute-start | bytes 786440 | tf_op jit(solution)/shard_map/ppermute | solution.py:21
  23.8 1.9 collective-permute-start.4
  25.7 2.0 fusion.150
  28.9 1.0 copy.44
  30.0 1.3 collective-permute-start.5
  31.3 1.1 collective-permute-done.2
  32.4 1.6 collective-permute-done.3
  34.0 8.2 %collective-permute-done.4 = bf16[2,128,512]{2,1,0:T(8,128)(2,1)S(1)} collective-permute-done((bf16[2,128,512]{2,1,0:T(8,128)(2,1)S(1)}, bf16[2,128,512]{2,1,0:T(8,128)(2,1)S(1)}, u32[]{:S(2)}, u32[]{:S(2)}) %collective-permute-start.4) | collective-permute-done | bytes 262176 | tf_op jit(solution)/shard_map/ppermute | solution.py:21
  42.2 1.0 fusion.146
  44.1 1.0 reshape_squeeze.9
  45.1 1.0 bitcast_reduce_fusion
  46.2 0.8 fusion.1
  47.0 0.8 fusion.3
  47.8 2.4 copy.45
  50.2 3.0 %reshape_squeeze.11 = bf16[896,8,64]{0,2,1:T(8,128)(2,1)} reshape(bf16[7,1,128,512]{2,0,3,1:T(8,128)(2,1)} %copy.45) | data formatting | bytes 1835008 | tf_op jit(solution)/shard_map/reshape;squeeze | solution.py:78
  53.4 1.7 convolution_convert_fusion
  55.4 8.2 %collective-permute-start.7 = (bf16[15,1024]{1,0:T(8,128)(2,1)S(1)}, bf16[15,1024]{1,0:T(8,128)(2,1)S(1)}, u32[]{:S(2)}, u32[]{:S(2)}) collective-permute-start(bf16[15,1024]{1,0:T(8,128)(2,1)S(1)} %get-tuple-element.66), channel_id=1, source_target_pairs={{2,0},{4,2},{6,4},{8,6},{10,8},{12,10},{14,12},{3,1},{5,3},{7,5},{... | collective-permute-start | bytes 92168 | tf_op jit(solution)/shard_map/ppermute | solution.py:34
  63.6 1.9 collective-permute-start.6
  65.6 1.1 fusion.151
  66.7 3.6 %collective-permute-done.6 = bf16[15,1024]{1,0:T(8,128)(2,1)S(1)} collective-permute-done((bf16[15,1024]{1,0:T(8,128)(2,1)S(1)}, bf16[15,1024]{1,0:T(8,128)(2,1)S(1)}, u32[]{:S(2)}, u32[]{:S(2)}) %collective-permute-start.6) | collective-permute-done | bytes 30752 | tf_op jit(solution)/shard_map/ppermute | solution.py:32
  70.5 4.1 %fusion.84 = (f32[1024]{0:T(1024)}, f32[1024]{0:T(1024)}, f32[1024]{0:T(1024)}, f32[1024]{0:T(1024)}, f32[1024]{0:T(1024)}, /*index=5*/f32[1024]{0:T(1024)}, f32...) fusion(bf16[15,1024]{1,0:T(8,128)(2,1)S(1)} %collective-permute-done.7, ...), kind=kLoop, calls=%fused_computation.216 | loop fusion | flops 31841280 | bytes 1011712 | tf_op jit(solution)/shard_map/reduce_sum | solution.py:115
  74.6 1.9 collective-permute-start.9
  76.5 4.8 %collective-permute-start.8 = (bf16[15,1024]{1,0:T(8,128)(2,1)S(1)}, bf16[15,1024]{1,0:T(8,128)(2,1)S(1)}, u32[]{:S(2)}, u32[]{:S(2)}) collective-permute-start(bf16[15,1024]{1,0:T(8,128)(2,1)S(1)} %get-tuple-element.63), channel_id=1, source_target_pairs={{2,0},{4,2},{6,4},{8,6},{10,8},{12,10},{14,12},{3,1},{5,3},{7,5},{... | collective-permute-start | bytes 92168 | tf_op jit(solution)/shard_map/ppermute | solution.py:34
  81.4 1.6 collective-permute-done.8
  82.9 2.5 fusion.37
  86.2 1.7 fusion.152
  88.2 2.1 fusion.67
  90.3 2.2 fusion.83
  92.5 2.4 fusion.68
  94.9 5.5 %stack.167 = f32[31,1024]{1,0:T(8,128)} concatenate(f32[1,1024]{1,0:T(1,128)} %bitcast.243, f32[1,1024]{1,0:T(1,128)} %bitcast.245, f32[1,1024]{1,0:T(1,128)} %bitcast.244, f32[1,1024]{1,0:T(1,128)} %bitcast.246, f32[1,1024]{1,0:T(1,128)} %bitcast.255, f32[1,1024]{1,0:T(1,128)} %bitcast.256, f32[1,1024]{1,0:T(1,128)} %bitcast.257, f32[1,1024]{1,0:T(1,128)} %bitcast.258, ...), dimensions={0} | concatenate | bytes 253952 | tf_op jit(solution)/shard_map/stack | solution.py:119
  100.4 1.4 convolution_convert_fusion.1
  102.0 2.1 multiply_convert_fusion
  104.2 1.2 copy-done.1
  105.4 2.1 multiply_bitcast_fusion
  107.5 2.7 %stack_reshape.6 = f32[7,1,128,512]{2,0,3,1:T(8,128)} reshape(f32[896,8,64]{0,2,1:T(8,128)} %multiply_bitcast_fusion) | data formatting | bytes 3670016 | tf_op jit(solution)/shard_map/stack;reshape | solution.py:155
  110.2 2.1 convolution_bitcast_fusion
  112.3 2.9 %stack_reshape.7 = f32[7,1,128,512]{2,0,3,1:T(8,128)} reshape(f32[896,8,64]{0,2,1:T(8,128)} %convolution_bitcast_fusion) | data formatting | bytes 3670016 | tf_op jit(solution)/shard_map/stack;reshape | solution.py:155
  115.2 1.5 constant_dynamic-update-slice_fusion.3
  116.7 1.0 copy-done.4
  117.6 1.4 constant_dynamic-update-slice_fusion.2
  119.1 30.6 %reduce-scatter.2.cloned.1.call-done = f32[32,1024]{1,0:T(8,128)} async-done(((f32[512,1024]{1,0:T(8,128)}), f32[32,1024]{1,0:T(8,128)}) %reduce-scatter.2.cloned.1.call-update) | async-done | bytes 131088 | tf_op jit(solution)/shard_map/reduce_scatter | solution.py:126
  149.7 1.5 convert_element_type.366
  151.3 15.1 %fusion.145 = (f32[1,2,128,512]{2,0,3,1:T(1,128)S(1)}, f32[1,2,128,512]{2,0,3,1:T(1,128)}, f32[1,2,128,512]{2,0,3,1:T(1,128)S(1)}, f32[1,2,128,512]{2,0,3,1:T(1,...) fusion(f32[7,2,128,512]{2,0,3,1:T(8,128)} %constant_dynamic-update-slice_fu, ...), kind=kLoop, calls=%fused_computation.316 | loop fusion | bytes 7340032 | tf_op jit(solution)/shard_map/slice | solution.py:51
  166.4 3.5 %collective-permute-start.15 = (f32[2,128,512]{1,2,0:T(8,128)S(1)}, f32[2,128,512]{1,2,0:T(8,128)S(1)}, u32[]{:S(2)}, u32[]{:S(2)}) collective-permute-start(f32[2,128,512]{1,2,0:T(8,128)S(1)} %bitcast.167), channel_id=1, source_target_pairs={{0,6},{2,8},{4,10},{6,12},{8,14},{1,7},{3,9},{5,11},{7,13},{9,15},... | collective-permute-start | bytes 1572872 | tf_op jit(solution)/shard_map/ppermute | solution.py:21
  169.9 2.3 collective-permute-start.14
  172.2 3.0 %collective-permute-start.13 = (f32[2,128,512]{1,2,0:T(8,128)}, f32[2,128,512]{1,2,0:T(8,128)}, u32[]{:S(2)}, u32[]{:S(2)}) collective-permute-start(f32[2,128,512]{1,2,0:T(8,128)} %bitcast.55), channel_id=1, source_target_pairs={{0,2},{2,4},{4,6},{6,8},{8,10},{10,12},{12,14},{1,3},{3,5},{5,7},{... | collective-permute-start | bytes 1572872 | tf_op jit(solution)/shard_map/ppermute | solution.py:21
  175.2 4.2 %collective-permute-start.12 = (f32[2,128,512]{1,2,0:T(8,128)S(1)}, f32[2,128,512]{1,2,0:T(8,128)}, u32[]{:S(2)}, u32[]{:S(2)}) collective-permute-start(f32[2,128,512]{1,2,0:T(8,128)S(1)} %bitcast.166), channel_id=1, source_target_pairs={{2,0},{4,2},{6,4},{8,6},{10,8},{12,10},{14,12},{3,1},{5,3},{7,5},{... | collective-permute-start | bytes 1572872 | tf_op jit(solution)/shard_map/ppermute | solution.py:21
  179.4 2.7 %collective-permute-start.11 = (f32[2,128,512]{1,2,0:T(8,128)S(1)}, f32[2,128,512]{1,2,0:T(8,128)}, u32[]{:S(2)}, u32[]{:S(2)}) collective-permute-start(f32[2,128,512]{1,2,0:T(8,128)S(1)} %bitcast.165), channel_id=1, source_target_pairs={{4,0},{6,2},{8,4},{10,6},{12,8},{14,10},{5,1},{7,3},{9,5},{11,7},{... | collective-permute-start | bytes 1572872 | tf_op jit(solution)/shard_map/ppermute | solution.py:21
  182.1 6.7 %collective-permute-done.15 = f32[2,128,512]{1,2,0:T(8,128)S(1)} collective-permute-done((f32[2,128,512]{1,2,0:T(8,128)S(1)}, f32[2,128,512]{1,2,0:T(8,128)S(1)}, u32[]{:S(2)}, u32[]{:S(2)}) %collective-permute-start.15) | collective-permute-done | bytes 524320 | tf_op jit(solution)/shard_map/ppermute | solution.py:21
  188.8 1.3 collective-permute-start.10
  190.6 0.8 copy.58
  191.4 9.6 %collective-permute-done.14 = f32[2,128,512]{1,2,0:T(8,128)} collective-permute-done((f32[2,128,512]{1,2,0:T(8,128)}, f32[2,128,512]{1,2,0:T(8,128)}, u32[]{:S(2)}, u32[]{:S(2)}) %collective-permute-start.14) | collective-permute-done | bytes 524320 | tf_op jit(solution)/shard_map/ppermute | solution.py:21
  201.0 18.6 %collective-permute-done.13 = f32[2,128,512]{1,2,0:T(8,128)} collective-permute-done((f32[2,128,512]{1,2,0:T(8,128)}, f32[2,128,512]{1,2,0:T(8,128)}, u32[]{:S(2)}, u32[]{:S(2)}) %collective-permute-start.13) | collective-permute-done | bytes 524320 | tf_op jit(solution)/shard_map/ppermute | solution.py:21
  219.6 2.1 collective-permute-done.11
  221.7 2.0 add_convert_fusion
  223.7 0.8 copy.59
  225.3 2.4 reduce_sum.339
  227.7 29.4 %all-gather.5.cloned.1.call-done = bf16[512,1024]{1,0:T(8,128)(2,1)} async-done(((bf16[32,1024]{1,0:T(8,128)(2,1)}), bf16[512,1024]{1,0:T(8,128)(2,1)}) %all-gather.5.cloned.1.call-update) | async-done | bytes 1048592 | tf_op jit(solution)/shard_map/all_gather | solution.py:127
  257.1 2.3 copy.82
  (99 shorter events, 4.4 us)
Async XLA Ops:
  7.2 47.9 %copy-start = (bf16[512,1024]{1,0:T(8,128)(2,1)S(1)}, bf16[512,1024]{1,0:T(8,128)(2,1)}, u32[]{:S(2)}) copy-start(bf16[512,1024]{1,0:T(8,128)(2,1)} %param.11) | copy-start | bytes 3145732
  7.2 142.5 %reduce-scatter.2.cloned.1.call-start = ((), (), s32[]{:S(2)}) async-start(), calls=%async_computation.1 | async-start | bytes 2228224 | tf_op jit(solution)/shard_map/reduce_scatter | solution.py:126
  9.1 20.8 %collective-permute-start = (bf16[2,128,512]{2,1,0:T(8,128)(2,1)S(1)}, bf16[2,128,512]{2,1,0:T(8,128)(2,1)S(1)}, u32[]{:S(2)}, u32[]{:S(2)}) collective-permute-start(bf16[2,128,512]{2,1,0:T(8,128)(2,1)S(1)} %constant_dynamic-update-slice_fusion), channel_id=1, source_target_pairs={{0,6},{2,8},{4,10},{6,12},{8,14},{1,7},{3,9},{5,11},{7,13},{9,15},... | collective-permute-start | bytes 786440 | tf_op jit(solution)/shard_map/ppermute | solution.py:21
  13.6 17.7 %collective-permute-start.1 = (bf16[2,128,512]{2,1,0:T(8,128)(2,1)S(1)}, bf16[2,128,512]{2,1,0:T(8,128)(2,1)S(1)}, u32[]{:S(2)}, u32[]{:S(2)}) collective-permute-start(bf16[2,128,512]{2,1,0:T(8,128)(2,1)S(1)} %constant_dynamic-update-slice_fusion), channel_id=1, source_target_pairs={{0,4},{2,6},{4,8},{6,10},{8,12},{10,14},{1,5},{3,7},{5,9},{7,11},{... | collective-permute-start | bytes 786440 | tf_op jit(solution)/shard_map/ppermute | solution.py:21
  17.1 15.3 %collective-permute-start.2 = (bf16[2,128,512]{2,1,0:T(8,128)(2,1)S(1)}, bf16[2,128,512]{2,1,0:T(8,128)(2,1)S(1)}, u32[]{:S(2)}, u32[]{:S(2)}) collective-permute-start(bf16[2,128,512]{2,1,0:T(8,128)(2,1)S(1)} %constant_dynamic-update-slice_fusion), channel_id=1, source_target_pairs={{0,2},{2,4},{4,6},{6,8},{8,10},{10,12},{12,14},{1,3},{3,5},{5,7},{... | collective-permute-start | bytes 786440 | tf_op jit(solution)/shard_map/ppermute | solution.py:21
  19.0 15.0 %collective-permute-start.3 = (bf16[2,128,512]{2,1,0:T(8,128)(2,1)S(1)}, bf16[2,128,512]{2,1,0:T(8,128)(2,1)S(1)}, u32[]{:S(2)}, u32[]{:S(2)}) collective-permute-start(bf16[2,128,512]{2,1,0:T(8,128)(2,1)S(1)} %constant_dynamic-update-slice_fusion), channel_id=1, source_target_pairs={{2,0},{4,2},{6,4},{8,6},{10,8},{12,10},{14,12},{3,1},{5,3},{7,5},{... | collective-permute-start | bytes 786440 | tf_op jit(solution)/shard_map/ppermute | solution.py:21
  23.8 18.4 %collective-permute-start.4 = (bf16[2,128,512]{2,1,0:T(8,128)(2,1)S(1)}, bf16[2,128,512]{2,1,0:T(8,128)(2,1)S(1)}, u32[]{:S(2)}, u32[]{:S(2)}) collective-permute-start(bf16[2,128,512]{2,1,0:T(8,128)(2,1)S(1)} %constant_dynamic-update-slice_fusion), channel_id=1, source_target_pairs={{4,0},{6,2},{8,4},{10,6},{12,8},{14,10},{5,1},{7,3},{9,5},{11,7},{... | collective-permute-start | bytes 786440 | tf_op jit(solution)/shard_map/ppermute | solution.py:21
  29.9 15.2 %copy-start.8 = (bf16[1,128,512]{1,2,0:T(8,128)(2,1)}, bf16[1,128,512]{1,2,0:T(8,128)(2,1)S(1)}, u32[]{:S(2)}) copy-start(bf16[1,128,512]{1,2,0:T(8,128)(2,1)S(1)} %copy.44) | copy-start | bytes 393220
  30.0 12.3 %collective-permute-start.5 = (bf16[2,128,512]{2,1,0:T(8,128)(2,1)S(1)}, bf16[2,128,512]{2,1,0:T(8,128)(2,1)S(1)}, u32[]{:S(2)}, u32[]{:S(2)}) collective-permute-start(bf16[2,128,512]{2,1,0:T(8,128)(2,1)S(1)} %constant_dynamic-update-slice_fusion), channel_id=1, source_target_pairs={{6,0},{8,2},{10,4},{12,6},{14,8},{7,1},{9,3},{11,5},{13,7},{15,9},... | collective-permute-start | bytes 786440 | tf_op jit(solution)/shard_map/ppermute | solution.py:21
  45.1 1.1 copy-start.5
  53.2 1.8 copy-start.33
  53.2 17.1 %copy-start.10 = (bf16[1,128,1024]{2,1,0:T(8,128)(2,1)S(1)}, bf16[1,128,1024]{2,1,0:T(8,128)(2,1)}, u32[]{:S(2)}) copy-start(bf16[1,128,1024]{2,1,0:T(8,128)(2,1)} %param.10) | copy-start | bytes 786436
  53.2 17.1 %copy-start.14 = (f32[1,1024]{1,0:T(1,128)S(1)}, f32[1,1024]{1,0:T(1,128)}, u32[]{:S(2)}) copy-start(f32[1,1024]{1,0:T(1,128)} %get-tuple-element.71) | copy-start | bytes 12292
  53.2 17.1 %copy-start.15 = (f32[1,1024]{1,0:T(1,128)S(1)}, f32[1,1024]{1,0:T(1,128)}, u32[]{:S(2)}) copy-start(f32[1,1024]{1,0:T(1,128)} %get-tuple-element.72) | copy-start | bytes 12292
  53.2 17.1 %copy-start.16 = (f32[1,1024]{1,0:T(1,128)S(1)}, f32[1,1024]{1,0:T(1,128)}, u32[]{:S(2)}) copy-start(f32[1,1024]{1,0:T(1,128)} %get-tuple-element.73) | copy-start | bytes 12292
  53.2 17.1 %copy-start.17 = (f32[1,1024]{1,0:T(1,128)S(1)}, f32[1,1024]{1,0:T(1,128)}, u32[]{:S(2)}) copy-start(f32[1,1024]{1,0:T(1,128)} %get-tuple-element.74) | copy-start | bytes 12292
  53.2 17.1 %copy-start.18 = (f32[1,1024]{1,0:T(1,128)S(1)}, f32[1,1024]{1,0:T(1,128)}, u32[]{:S(2)}) copy-start(f32[1,1024]{1,0:T(1,128)} %get-tuple-element.75) | copy-start | bytes 12292
  53.3 17.1 %copy-start.19 = (f32[1,1024]{1,0:T(1,128)S(1)}, f32[1,1024]{1,0:T(1,128)}, u32[]{:S(2)}) copy-start(f32[1,1024]{1,0:T(1,128)} %get-tuple-element.76) | copy-start | bytes 12292
  53.3 17.1 %copy-start.20 = (f32[1,1024]{1,0:T(1,128)S(1)}, f32[1,1024]{1,0:T(1,128)}, u32[]{:S(2)}) copy-start(f32[1,1024]{1,0:T(1,128)} %get-tuple-element.77) | copy-start | bytes 12292
  53.3 17.1 %copy-start.21 = (f32[1,1024]{1,0:T(1,128)S(1)}, f32[1,1024]{1,0:T(1,128)}, u32[]{:S(2)}) copy-start(f32[1,1024]{1,0:T(1,128)} %get-tuple-element.78) | copy-start | bytes 12292
  53.3 17.1 %copy-start.22 = (f32[1,1024]{1,0:T(1,128)S(1)}, f32[1,1024]{1,0:T(1,128)}, u32[]{:S(2)}) copy-start(f32[1,1024]{1,0:T(1,128)} %get-tuple-element.79) | copy-start | bytes 12292
  53.3 17.1 %copy-start.23 = (f32[1,1024]{1,0:T(1,128)S(1)}, f32[1,1024]{1,0:T(1,128)}, u32[]{:S(2)}) copy-start(f32[1,1024]{1,0:T(1,128)} %get-tuple-element.80) | copy-start | bytes 12292
  53.3 17.1 %copy-start.24 = (f32[1,1024]{1,0:T(1,128)S(1)}, f32[1,1024]{1,0:T(1,128)}, u32[]{:S(2)}) copy-start(f32[1,1024]{1,0:T(1,128)} %get-tuple-element.81) | copy-start | bytes 12292
  53.3 17.1 %copy-start.25 = (f32[1,1024]{1,0:T(1,128)S(1)}, f32[1,1024]{1,0:T(1,128)}, u32[]{:S(2)}) copy-start(f32[1,1024]{1,0:T(1,128)} %get-tuple-element.82) | copy-start | bytes 12292
  53.3 17.1 %copy-start.26 = (f32[1,1024]{1,0:T(1,128)S(1)}, f32[1,1024]{1,0:T(1,128)}, u32[]{:S(2)}) copy-start(f32[1,1024]{1,0:T(1,128)} %get-tuple-element.83) | copy-start | bytes 12292
  53.3 17.1 %copy-start.27 = (f32[1,1024]{1,0:T(1,128)S(1)}, f32[1,1024]{1,0:T(1,128)}, u32[]{:S(2)}) copy-start(f32[1,1024]{1,0:T(1,128)} %get-tuple-element.84) | copy-start | bytes 12292
  53.3 17.1 %copy-start.28 = (f32[1,1024]{1,0:T(1,128)S(1)}, f32[1,1024]{1,0:T(1,128)}, u32[]{:S(2)}) copy-start(f32[1,1024]{1,0:T(1,128)} %get-tuple-element.85) | copy-start | bytes 12292
  55.4 11.3 %collective-permute-start.7 = (bf16[15,1024]{1,0:T(8,128)(2,1)S(1)}, bf16[15,1024]{1,0:T(8,128)(2,1)S(1)}, u32[]{:S(2)}, u32[]{:S(2)}) collective-permute-start(bf16[15,1024]{1,0:T(8,128)(2,1)S(1)} %get-tuple-element.66), channel_id=1, source_target_pairs={{2,0},{4,2},{6,4},{8,6},{10,8},{12,10},{14,12},{3,1},{5,3},{7,5},{... | collective-permute-start | bytes 92168 | tf_op jit(solution)/shard_map/ppermute | solution.py:34
  63.6 6.7 %collective-permute-start.6 = (bf16[15,1024]{1,0:T(8,128)(2,1)S(1)}, bf16[15,1024]{1,0:T(8,128)(2,1)S(1)}, u32[]{:S(2)}, u32[]{:S(2)}) collective-permute-start(bf16[15,1024]{1,0:T(8,128)(2,1)S(1)} %get-tuple-element.65), channel_id=1, source_target_pairs={{0,2},{2,4},{4,6},{6,8},{8,10},{10,12},{12,14},{1,3},{3,5},{5,7},{... | collective-permute-start | bytes 92168 | tf_op jit(solution)/shard_map/ppermute | solution.py:32
  66.7 18.8 %copy-start.13 = (bf16[15,1024]{1,0:T(8,128)(2,1)}, bf16[15,1024]{1,0:T(8,128)(2,1)S(1)}, u32[]{:S(2)}) copy-start(bf16[15,1024]{1,0:T(8,128)(2,1)S(1)} %collective-permute-done.7) | copy-start | bytes 92164
  70.3 15.1 %copy-start.12 = (bf16[15,1024]{1,0:T(8,128)(2,1)}, bf16[15,1024]{1,0:T(8,128)(2,1)S(1)}, u32[]{:S(2)}) copy-start(bf16[15,1024]{1,0:T(8,128)(2,1)S(1)} %collective-permute-done.6) | copy-start | bytes 92164
  74.6 6.8 %collective-permute-start.9 = (bf16[15,1024]{1,0:T(8,128)(2,1)S(1)}, bf16[15,1024]{1,0:T(8,128)(2,1)S(1)}, u32[]{:S(2)}, u32[]{:S(2)}) collective-permute-start(bf16[15,1024]{1,0:T(8,128)(2,1)S(1)} %get-tuple-element.64), channel_id=1, source_target_pairs={{0,2},{2,4},{4,6},{6,8},{8,10},{10,12},{12,14},{1,3},{3,5},{5,7},{... | collective-permute-start | bytes 92168 | tf_op jit(solution)/shard_map/ppermute | solution.py:32
  76.5 6.4 %collective-permute-start.8 = (bf16[15,1024]{1,0:T(8,128)(2,1)S(1)}, bf16[15,1024]{1,0:T(8,128)(2,1)S(1)}, u32[]{:S(2)}, u32[]{:S(2)}) collective-permute-start(bf16[15,1024]{1,0:T(8,128)(2,1)S(1)} %get-tuple-element.63), channel_id=1, source_target_pairs={{2,0},{4,2},{6,4},{8,6},{10,8},{12,10},{14,12},{3,1},{5,3},{7,5},{... | collective-permute-start | bytes 92168 | tf_op jit(solution)/shard_map/ppermute | solution.py:34
  85.5 0.7 copy-start.7
  87.9 6.9 %copy-start.29 = (f32[1024]{0:T(1024)S(1)}, f32[1024]{0:T(1024)}, u32[]{:S(2)}) copy-start(f32[1024]{0:T(1024)} %get-tuple-element.20) | copy-start | bytes 12292
  87.9 6.9 %copy-start.30 = (f32[1024]{0:T(1024)S(1)}, f32[1024]{0:T(1024)}, u32[]{:S(2)}) copy-start(f32[1024]{0:T(1024)} %get-tuple-element.21) | copy-start | bytes 12292
  88.0 6.9 %copy-start.31 = (f32[1024]{0:T(1024)S(1)}, f32[1024]{0:T(1024)}, u32[]{:S(2)}) copy-start(f32[1024]{0:T(1024)} %get-tuple-element.22) | copy-start | bytes 12292
  88.0 6.9 %copy-start.32 = (f32[1024]{0:T(1024)S(1)}, f32[1024]{0:T(1024)}, u32[]{:S(2)}) copy-start(f32[1024]{0:T(1024)} %get-tuple-element.23) | copy-start | bytes 12292
  88.0 137.3 %all-gather.7.cloned.1.call-start = ((), (), s32[]{:S(2)}) async-start(), calls=%async_computation.3 | async-start | bytes 2228224 | tf_op jit(solution)/shard_map/all_gather | solution.py:14
  100.4 156.7 %all-gather.5.cloned.1.call-start = ((), (), s32[]{:S(2)}) async-start(), calls=%async_computation.2 | async-start | bytes 1114112 | tf_op jit(solution)/shard_map/all_gather | solution.py:127
  102.0 3.4 %copy-start.9 = (bf16[1,128,512]{1,2,0:T(8,128)(2,1)S(1)}, bf16[1,128,512]{1,2,0:T(8,128)(2,1)}, u32[]{:S(2)}) copy-start(bf16[1,128,512]{1,2,0:T(8,128)(2,1)} %copy-done.8) | copy-start | bytes 393220
  104.2 1.2 copy-start.1
  112.3 2.9 %copy-start.3 = (f32[7,1,128,512]{2,0,3,1:T(8,128)S(1)}, f32[7,1,128,512]{2,0,3,1:T(8,128)}, u32[]{:S(2)}) copy-start(f32[7,1,128,512]{2,0,3,1:T(8,128)} %stack_reshape.6) | copy-start | bytes 5505028
  115.2 2.4 copy-start.4
  151.2 38.9 %copy-start.2 = (bf16[8,128,896]{1,2,0:T(8,128)(2,1)S(1)}, bf16[8,128,896]{1,2,0:T(8,128)(2,1)}, u32[]{:S(2)}) copy-start(bf16[8,128,896]{1,2,0:T(8,128)(2,1)} %copy-done.1) | copy-start | bytes 5505028
  151.3 38.9 %copy-start.6 = (bf16[896,8,64]{0,2,1:T(8,128)(2,1)S(1)}, bf16[896,8,64]{0,2,1:T(8,128)(2,1)}, u32[]{:S(2)}) copy-start(bf16[896,8,64]{0,2,1:T(8,128)(2,1)} %copy-done.5) | copy-start | bytes 2752516
  166.4 22.4 %collective-permute-start.15 = (f32[2,128,512]{1,2,0:T(8,128)S(1)}, f32[2,128,512]{1,2,0:T(8,128)S(1)}, u32[]{:S(2)}, u32[]{:S(2)}) collective-permute-start(f32[2,128,512]{1,2,0:T(8,128)S(1)} %bitcast.167), channel_id=1, source_target_pairs={{0,6},{2,8},{4,10},{6,12},{8,14},{1,7},{3,9},{5,11},{7,13},{9,15},... | collective-permute-start | bytes 1572872 | tf_op jit(solution)/shard_map/ppermute | solution.py:21
  169.9 31.1 %collective-permute-start.14 = (f32[2,128,512]{1,2,0:T(8,128)}, f32[2,128,512]{1,2,0:T(8,128)}, u32[]{:S(2)}, u32[]{:S(2)}) collective-permute-start(f32[2,128,512]{1,2,0:T(8,128)} %bitcast.56), channel_id=1, source_target_pairs={{0,4},{2,6},{4,8},{6,10},{8,12},{10,14},{1,5},{3,7},{5,9},{7,11},{... | collective-permute-start | bytes 1572872 | tf_op jit(solution)/shard_map/ppermute | solution.py:21
  172.2 47.5 %collective-permute-start.13 = (f32[2,128,512]{1,2,0:T(8,128)}, f32[2,128,512]{1,2,0:T(8,128)}, u32[]{:S(2)}, u32[]{:S(2)}) collective-permute-start(f32[2,128,512]{1,2,0:T(8,128)} %bitcast.55), channel_id=1, source_target_pairs={{0,2},{2,4},{4,6},{6,8},{8,10},{10,12},{12,14},{1,3},{3,5},{5,7},{... | collective-permute-start | bytes 1572872 | tf_op jit(solution)/shard_map/ppermute | solution.py:21
  175.2 44.4 %collective-permute-start.12 = (f32[2,128,512]{1,2,0:T(8,128)S(1)}, f32[2,128,512]{1,2,0:T(8,128)}, u32[]{:S(2)}, u32[]{:S(2)}) collective-permute-start(f32[2,128,512]{1,2,0:T(8,128)S(1)} %bitcast.166), channel_id=1, source_target_pairs={{2,0},{4,2},{6,4},{8,6},{10,8},{12,10},{14,12},{3,1},{5,3},{7,5},{... | collective-permute-start | bytes 1572872 | tf_op jit(solution)/shard_map/ppermute | solution.py:21
  179.4 42.3 %collective-permute-start.11 = (f32[2,128,512]{1,2,0:T(8,128)S(1)}, f32[2,128,512]{1,2,0:T(8,128)}, u32[]{:S(2)}, u32[]{:S(2)}) collective-permute-start(f32[2,128,512]{1,2,0:T(8,128)S(1)} %bitcast.165), channel_id=1, source_target_pairs={{4,0},{6,2},{8,4},{10,6},{12,8},{14,10},{5,1},{7,3},{9,5},{11,7},{... | collective-permute-start | bytes 1572872 | tf_op jit(solution)/shard_map/ppermute | solution.py:21
  188.8 1.8 copy-start.11
  188.8 32.9 %collective-permute-start.10 = (f32[2,128,512]{1,2,0:T(8,128)S(1)}, f32[2,128,512]{1,2,0:T(8,128)}, u32[]{:S(2)}, u32[]{:S(2)}) collective-permute-start(f32[2,128,512]{1,2,0:T(8,128)S(1)} %bitcast.164), channel_id=1, source_target_pairs={{6,0},{8,2},{10,4},{12,6},{14,8},{7,1},{9,3},{11,5},{13,7},{15,9},... | collective-permute-start | bytes 1572872 | tf_op jit(solution)/shard_map/ppermute | solution.py:21
Sparse Core Ops, SparseCore 0:
  88.1 61.5 reduce-scatter.1
  151.8 67.2 all-gather.6
  221.3 35.7 all-gather.4
